TPU v7x, 32 devices: a whole 2x2x4 slice. The times are simulated.
32 devices in a mesh: req: 2 (over x), seq: 16 (over z, y, core).
Axes of the slice: x: 2, y: 2, z: 4, core: 2. Of those that a mesh axis runs over, the one named last changes fastest.
Arguments:
- states: bfloat16 [4, 4, 4544], P(None, 'req', 'seq'), may hold values from -6 to 6
- kv_cache: bfloat16 [4, 8192, 128], P('req', 'seq'), may hold values from -48 to 48, as said below
- lengths: int32 [4], replicated, may hold values from 1 to 8188, as said below
- placement: int32 [4], replicated, may hold values from 0 to 3, each once
- norm_gain: bfloat16 [4544], replicated, may hold values from 0.25 to 1.75
- norm_bias: bfloat16 [4544], replicated, may hold values from -1.5 to 1.5
- w_query: bfloat16 [4544, 4544], P('req', 'seq'), may hold values from -0.09375 to 0.09375
- w_keyval: bfloat16 [4544, 128], P('req'), may hold values from -0.09375 to 0.09375
- w_out: bfloat16 [4544, 4544], P('seq', 'req'), may hold values from -0.09375 to 0.09375
- w_up: bfloat16 [4544, 18176], P('req', 'seq'), may hold values from -0.09375 to 0.09375
- w_down: bfloat16 [18176, 4544], P('seq', 'req'), may hold values from -0.046875 to 0.046875
Outputs:
- new_states: bfloat16 [4, 4, 4544], P(None, 'req', 'seq')
- new_cache: bfloat16 [4, 8192, 128], P('req', 'seq')
Inputs may be any that keep to these rules, and one draw needn't show every extreme that they name: Request r's cache holds its first lengths[r] positions; some request has exactly 8188. `kv_cache`: row i is the cache of request placement[i]; positions at or beyond that request's length hold arbitrary values. `placement`: each request is served by exactly one slot.
All inputs are finite; a program needn't handle non-finite values.
Results may differ from a plain program's by a relative error of at most 0.012.
The roundings to bfloat16 on the way count: a program that leaves them out, or rounds other values in their place, can miss the bound.
Values may be sent and summed in bfloat16 or wider, within the bound.
No kernel may reach another device: no remote copies, remote signals or barrier semaphores. Data moves between devices by JAX's collectives and lax.ppermute only.
A program may use at most 192 MiB of HBM per device.

v0:
```python
import jax
import jax.numpy as jnp
from jax import lax
from jax.sharding import PartitionSpec as P

EPSILON = 1e-05
NEGATIVE = -1e30
ALL = ("req", "seq")


def layer_norm(row_block, norm_gain, norm_bias):
    values = row_block.astype(jnp.float32)
    average = jnp.mean(values, axis=-1, keepdims=True)
    centered = values - average
    spread = jnp.mean(centered * centered, axis=-1, keepdims=True)
    scaled = centered * lax.rsqrt(spread + EPSILON)
    return (scaled * norm_gain.astype(jnp.float32) + norm_bias.astype(jnp.float32)).astype(
        jnp.bfloat16
    )


def rotate(vectors, positions):
    head_width = vectors.shape[-1]
    half_width = head_width // 2
    frequency = 10000.0 ** (-(jnp.arange(half_width, dtype=jnp.float32) * 2.0) / head_width)
    angles = positions.astype(jnp.float32)[:, None] * frequency[None, :]
    cosine = jnp.concatenate([jnp.cos(angles), jnp.cos(angles)], axis=-1)[:, None, :]
    sine_wave = jnp.concatenate([jnp.sin(angles), jnp.sin(angles)], axis=-1)[:, None, :]
    turned = jnp.concatenate([-vectors[..., half_width:], vectors[..., :half_width]], axis=-1)
    return vectors * cosine + turned * sine_wave


def shards(
    states,
    kv_cache,
    lengths,
    placement,
    norm_gain,
    norm_bias,
    w_query,
    w_keyval,
    w_out,
    w_up,
    w_down,
):
    steps = states.shape[0]
    group_rows = kv_cache.shape[0]
    seg_length = kv_cache.shape[1]
    head_width = kv_cache.shape[2] // 2
    model_width = norm_gain.shape[0]
    head_count = model_width // head_width
    slice_width = states.shape[2]
    part_width = w_query.shape[0]
    total = placement.shape[0]
    req_size = total // group_rows
    seq_size = model_width // slice_width
    rows = steps * total
    group_index = lax.axis_index("req")
    shard_index = lax.axis_index("seq")
    own_requests = lax.dynamic_slice_in_dim(placement, group_index * group_rows, group_rows, 0)
    slot_lengths = jnp.take(lengths, own_requests)
    step_offsets = jnp.arange(steps, dtype=jnp.int32)
    positions = slot_lengths[None, :] + step_offsets[:, None]
    every = lax.all_gather(states, ALL, axis=0, tiled=False)
    every = every.reshape(req_size, seq_size, steps, group_rows, slice_width)
    every = every.transpose(2, 0, 3, 1, 4).reshape(steps, total, model_width)
    current_all = jnp.take(every, placement, axis=1)
    normed = layer_norm(current_all.reshape(rows, model_width), norm_gain, norm_bias)
    normed_part = lax.dynamic_slice_in_dim(normed, group_index * part_width, part_width, 1)
    part_query = jnp.dot(normed_part, w_query, preferred_element_type=jnp.float32)
    part_keyval = jnp.dot(normed_part, w_keyval, preferred_element_type=jnp.float32)
    part_up = jnp.dot(normed_part, w_up, preferred_element_type=jnp.float32)
    first = lax.psum(jnp.concatenate([part_query, part_keyval, part_up], axis=1), "req")
    query_raw = first[:, :slice_width].astype(jnp.bfloat16).reshape(steps, total, slice_width)
    keyval = first[:, slice_width : slice_width + 2 * head_width].reshape(
        steps, total, 2 * head_width
    )
    up_part = first[:, slice_width + 2 * head_width :]
    own_query = lax.dynamic_slice_in_dim(query_raw, group_index * group_rows, group_rows, 1)
    query_all = lax.all_gather(own_query, "seq", axis=2, tiled=True)
    flat_positions = positions.reshape(-1)
    query_rows = rotate(
        query_all.astype(jnp.float32).reshape(steps * group_rows, head_count, head_width),
        flat_positions,
    ).astype(jnp.bfloat16)
    own_keyval = lax.dynamic_slice_in_dim(keyval, group_index * group_rows, group_rows, 1)
    own_keyval = own_keyval.reshape(steps * group_rows, 2 * head_width)
    new_key = rotate(own_keyval[:, None, :head_width], flat_positions)[:, 0, :]
    new_entry = jnp.concatenate([new_key, own_keyval[:, head_width:]], axis=-1).astype(jnp.bfloat16)
    new_entry = new_entry.reshape(steps, group_rows, 2 * head_width)
    local_slots = jnp.arange(seg_length, dtype=jnp.int32)
    global_positions = shard_index * seg_length + local_slots
    cache_now = kv_cache
    for step_index in range(steps):
        write_mask = global_positions[None, :] == positions[step_index][:, None]
        cache_now = jnp.where(write_mask[:, :, None], new_entry[step_index][:, None, :], cache_now)
    key_rows = cache_now[:, :, :head_width]
    value_rows = cache_now[:, :, head_width:]
    query_heads = (
        query_rows.reshape(steps, group_rows, head_count, head_width)
        .transpose(1, 0, 2, 3)
        .reshape(group_rows, steps * head_count, head_width)
    )
    scores = jnp.einsum(
        "gqd,gsd->gqs", query_heads, key_rows, preferred_element_type=jnp.float32
    ) * head_width ** (-0.5)
    valid = global_positions[None, None, :] <= positions.T[:, :, None]
    valid = jnp.broadcast_to(
        valid[:, :, None, :], (group_rows, steps, head_count, seg_length)
    ).reshape(group_rows, steps * head_count, seg_length)
    local_peak = jnp.max(jnp.where(valid, scores, NEGATIVE), axis=-1)
    weights = jnp.where(valid, jnp.exp(scores - local_peak[:, :, None]), 0.0)
    local_total = jnp.sum(weights, axis=-1)
    local_weighted = jnp.einsum(
        "gqs,gsd->gqd", weights, value_rows, preferred_element_type=jnp.float32
    )
    peak_buffer = jnp.full((total, steps * head_count), NEGATIVE, jnp.float32)
    peak_buffer = lax.dynamic_update_slice_in_dim(
        peak_buffer, local_peak, group_index * group_rows, 0
    )
    peak = lax.pmax(peak_buffer, ALL)
    own_peak = lax.dynamic_slice_in_dim(peak, group_index * group_rows, group_rows, 0)
    scale = jnp.exp(local_peak - own_peak)
    packed = jnp.concatenate(
        [local_weighted * scale[:, :, None], (local_total * scale)[:, :, None]], axis=-1
    )
    packed_buffer = jnp.zeros((total, steps * head_count, head_width + 1), jnp.float32)
    packed_buffer = lax.dynamic_update_slice_in_dim(
        packed_buffer, packed, group_index * group_rows, 0
    )
    summed = lax.psum(packed_buffer, ALL)
    mixed = summed[:, :, :head_width] / summed[:, :, head_width:]
    mixed = (
        mixed.reshape(total, steps, model_width)
        .transpose(1, 0, 2)
        .reshape(rows, model_width)
        .astype(jnp.bfloat16)
    )
    mixed_part = lax.dynamic_slice_in_dim(mixed, shard_index * slice_width, slice_width, 1)
    hidden = jax.nn.gelu(up_part, approximate=False).astype(jnp.bfloat16)
    partial_sum = jnp.dot(mixed_part, w_out, preferred_element_type=jnp.float32) + jnp.dot(
        hidden, w_down, preferred_element_type=jnp.float32
    )
    out_buffer = jnp.zeros((rows, model_width), jnp.float32)
    out_buffer = lax.dynamic_update_slice_in_dim(
        out_buffer, partial_sum, group_index * part_width, 1
    )
    branch = lax.psum(out_buffer, ALL).reshape(steps, total, model_width)
    inverse = jnp.zeros((total,), jnp.int32).at[placement].set(jnp.arange(total, dtype=jnp.int32))
    own_inverse = lax.dynamic_slice_in_dim(inverse, group_index * group_rows, group_rows, 0)
    own_branch = jnp.take(branch, own_inverse, axis=1)
    own_branch = lax.dynamic_slice_in_dim(own_branch, shard_index * slice_width, slice_width, 2)
    new_states = (states.astype(jnp.float32) + own_branch).astype(jnp.bfloat16)
    return (new_states, cache_now)


def solution(mesh):
    in_specs = (
        P(None, "req", "seq"),
        P("req", "seq", None),
        P(),
        P(),
        P(),
        P(),
        P("req", "seq"),
        P("req", None),
        P("seq", "req"),
        P("req", "seq"),
        P("seq", "req"),
    )
    out_specs = (P(None, "req", "seq"), P("req", "seq", None))
    return jax.shard_map(shards, mesh=mesh, in_specs=in_specs, out_specs=out_specs, check_vma=False)
```

profile of v0, /device:TPU:8, one launch (start us, length us, event | category | flops | bytes accessed | tf_op | source)
XLA Modules:
  0.0 437.4 jit_solution(13402356280962080718)
XLA Ops:
  7.2 0.8 compare_select_fusion.2
  8.0 0.7 compare_and_fusion
  8.6 0.8 dynamic-slice.1
  9.4 0.8 dynamic-slice.2
  10.2 38.8 %all-gather = bf16[128,2,284]{2,1,0:T(2,128)(2,1)S(1)} all-gather(bf16[4,2,284]{2,1,0:T(2,128)(2,1)} %param.11), channel_id=2, replica_groups=mesh['req'=2,'seq'=16] {'req','seq'}, dimensions={0}, use_global_device_ids=true | all-gather | bytes 149952 | tf_op jit(solution)/shard_map/all_gather | solution.py:64
  49.4 0.7 gather_fusion.1
  51.3 3.5 fusion.96
  55.1 0.4 fusion.95
  55.5 0.8 concatenate.40
  56.5 0.6 gather_fusion
  58.3 19.3 %all-reduce.4.cloned.1.call-done = f32[16,1548]{1,0:T(8,128)} async-done(((f32[16,1548]{1,0:T(8,128)}), f32[16,1548]{1,0:T(8,128)}) %all-reduce.4.cloned.1.call-update) | async-done | bytes 99088 | tf_op jit(solution)/shard_map/psum | solution.py:73
  77.6 0.8 slice.99
  78.4 0.7 slice.124
  79.4 32.2 %all_gather.11 = bf16[4,2,4544]{0,1,2:T(2,128)(2,1)} all-gather(bf16[4,2,284]{0,1,2:T(2,128)(2,1)S(1)} %copy.88), channel_id=1, replica_groups=mesh['req'=2,'seq'=16] {'seq'}, dimensions={2}, use_global_device_ids=true | all-gather | bytes 77248 | tf_op jit(solution)/shard_map/all_gather | solution.py:80
  111.6 5.2 %copy.73 = bf16[4,2,4544]{2,0,1:T(4,128)(2,1)S(1)} copy(bf16[4,2,4544]{0,1,2:T(2,128)(2,1)} %all_gather.11) | data formatting | bytes 145408 | tf_op jit(solution)/shard_map/all_gather | solution.py:80
  118.8 0.5 select_reduce_fusion
  119.3 41.3 %pmax.7 = f32[4,284]{1,0:T(4,128)S(1)} all-reduce(f32[4,284]{1,0:T(4,128)S(1)} %constant_dynamic-update-slice_fusion.1), channel_id=1, replica_groups=mesh['req'=2,'seq'=16] {'req','seq'}, use_global_device_ids=true, to_apply=%region_5.6 | all-reduce | flops 1136 | bytes 9088 | tf_op jit(solution)/shard_map/pmax | solution.py:121
  160.6 0.4 fusion
  161.0 0.4 convolution_multiply_fusion.1
  161.7 0.8 copy-done.2
  162.6 0.6 scatter_custom_fusion
  163.2 129.3 %all-reduce.6.cloned.1.call-done = f32[4,284,65]{2,1,0:T(8,128)} async-done(((f32[4,284,65]{2,1,0:T(8,128)}), f32[4,284,65]{2,1,0:T(8,128)}) %all-reduce.6.cloned.1.call-update) | async-done | bytes 295376 | tf_op jit(solution)/shard_map/psum | solution.py:131
  292.5 1.5 slice_reduce_fusion
  294.0 1.3 fusion.1
  295.6 0.4 fusion.55
  296.2 3.4 convolution_add_fusion
  299.7 1.3 dynamic_update_slice.11
  301.1 0.8 copy.84
  302.0 0.8 copy.86
  302.9 125.7 %all-reduce.8.cloned.1.call-done = f32[4,4,4544]{2,0,1:T(4,128)} async-done(((f32[4,4,4544]{2,0,1:T(4,128)}), f32[4,4,4544]{2,0,1:T(4,128)}) %all-reduce.8.cloned.1.call-update) | async-done | bytes 290832 | tf_op jit(solution)/shard_map/psum | solution.py:148
  428.5 1.6 gather_fusion.2
  430.2 0.6 copy.85
  (97 shorter events, 6.5 us)
Async XLA Ops:
  7.2 288.4 %copy-start = (bf16[284,2272]{1,0:T(8,128)(2,1)S(1)}, bf16[284,2272]{1,0:T(8,128)(2,1)}, u32[]{:S(2)}) copy-start(bf16[284,2272]{1,0:T(8,128)(2,1)} %param.19) | copy-start | bytes 3871492
  7.2 70.4 %all-reduce.4.cloned.1.call-start = ((), (), s32[]{:S(2)}) async-start(), calls=%async_computation | async-start | bytes 212992 | tf_op jit(solution)/shard_map/psum | solution.py:73
  51.3 3.5 copy-start.4
  51.3 3.8 copy-start.3
  54.8 1.6 copy-start.8
  54.8 1.7 copy-start.1
  55.1 2.6 copy-start.5
  56.3 236.2 %all-reduce.6.cloned.1.call-start = ((), (), s32[]{:S(2)}) async-start(), calls=%async_computation.1 | async-start | bytes 1179648 | tf_op jit(solution)/shard_map/psum | solution.py:131
  161.7 0.8 copy-start.2
  162.6 266.0 %all-reduce.8.cloned.1.call-start = ((), (), s32[]{:S(2)}) async-start(), calls=%async_computation.2 | async-start | bytes 589824 | tf_op jit(solution)/shard_map/psum | solution.py:148
  295.3 0.9 copy-start.6
  301.0 129.2 %copy-start.7 = (bf16[4,2,284]{2,1,0:T(2,128)(2,1)S(1)}, bf16[4,2,284]{2,1,0:T(2,128)(2,1)}, u32[]{:S(2)}) copy-start(bf16[4,2,284]{2,1,0:T(2,128)(2,1)} %param.11) | copy-start | bytes 13636
Sparse Core Ops, SparseCore 0:
  56.4 21.1 all-reduce.3
  162.7 129.7 all-reduce.5
  302.1 126.4 all-reduce.7
where the time goes:
time: 438 us; the launch traced here: 437 us
  waiting for transfers between devices  274 us (63%)
  blocking collectives  112 us (26%)
  local copies, waits for them, and re-layouts  22.3 us (5%)
  between operations  14.2 us (3%)
  matrix products  8.89 us (2%)
  other arithmetic  5.32 us (1%)
    psum x1, waiting for transfers between devices, shards(): summed = lax.psum(packed_buffer, ALL)  129 us
    psum x1, waiting for transfers between devices, shards(): branch = lax.psum(out_buffer, ALL).reshape(steps, total, model_width)  126 us
    pmax x1, blocking collectives, shards(): peak = lax.pmax(peak_buffer, ALL)  41.3 us
    all_gather x1, blocking collectives, shards(): every = lax.all_gather(states, ALL, axis=0, tiled=False)  38.8 us
    all_gather x1, blocking collectives, shards(): query_all = lax.all_gather(own_query, 'seq', axis=2, tiled=True)  32.2 us
    psum x1, waiting for transfers between devices, shards(): lax.psum(jnp.concatenate([part_query, part_keyval, part_up], axis=1), 'req')  19.3 us
  transfers between devices with their start and end apart: 3, of which 3 were waited for; matrix products, arithmetic and copies ran while one was open for 1% of the time, Pallas kernels for 0%

commit v1 on v0

--- a/solution.py
+++ b/solution.py
@@ -128,7 +128,7 @@
     packed_buffer = lax.dynamic_update_slice_in_dim(
         packed_buffer, packed, group_index * group_rows, 0
     )
-    summed = lax.psum(packed_buffer, ALL)
+    summed = jnp.sum(lax.all_gather(packed_buffer, ALL), axis=0)
     mixed = summed[:, :, :head_width] / summed[:, :, head_width:]
     mixed = (
         mixed.reshape(total, steps, model_width)

time: 438 us -> 410 us (0.936)
  waiting for transfers between devices: 274 us -> 242 us
  other arithmetic: 5.32 us -> 10.8 us
    psum x1 -> x0, waiting for transfers between devices: 129 us -> none  [shards(): summed = lax.psum(packed_buffer, ALL)]
    all_gather x0 -> x1, waiting for transfers between devices: none -> 97.1 us  [shards(): summed = jnp.sum(lax.all_gather(packed_buffer, ALL), axis=0)]
    reduce_sum x0 -> x1, other arithmetic: none -> 6.72 us  [shards(): summed = jnp.sum(lax.all_gather(packed_buffer, ALL), axis=0)]
where the time goes in v1:
time: 410 us; the launch traced here: 409 us
  waiting for transfers between devices  242 us (59%)
  blocking collectives  112 us (27%)
  local copies, waits for them, and re-layouts  21.2 us (5%)
  between operations  14.2 us (3%)
  other arithmetic  10.8 us (3%)
  matrix products  8.9 us (2%)
    psum x1, waiting for transfers between devices, shards(): branch = lax.psum(out_buffer, ALL).reshape(steps, total, model_width)  125 us
    all_gather x1, waiting for transfers between devices, shards(): summed = jnp.sum(lax.all_gather(packed_buffer, ALL), axis=0)  97.1 us
    pmax x1, blocking collectives, shards(): peak = lax.pmax(peak_buffer, ALL)  41.3 us
    all_gather x1, blocking collectives, shards(): every = lax.all_gather(states, ALL, axis=0, tiled=False)  38.8 us
    all_gather x1, blocking collectives, shards(): query_all = lax.all_gather(own_query, 'seq', axis=2, tiled=True)  32.2 us
    psum x1, waiting for transfers between devices, shards(): lax.psum(jnp.concatenate([part_query, part_keyval, part_up], axis=1), 'req')  19.3 us
  transfers between devices with their start and end apart: 3, of which 3 were waited for; matrix products, arithmetic and copies ran while one was open for 1% of the time, Pallas kernels for 0%

profile of v1, /device:TPU:8, one launch (start us, length us, event | category | flops | bytes accessed | tf_op | source)
XLA Modules:
  0.0 409.4 jit_solution(7489681770783762930)
XLA Ops:
  7.2 0.8 compare_select_fusion.2
  8.0 0.7 compare_and_fusion
  8.6 0.8 dynamic-slice.1
  9.4 0.8 dynamic-slice.2
  10.2 38.8 %all-gather = bf16[128,2,284]{2,1,0:T(2,128)(2,1)S(1)} all-gather(bf16[4,2,284]{2,1,0:T(2,128)(2,1)} %param.11), channel_id=2, replica_groups=mesh['req'=2,'seq'=16] {'req','seq'}, dimensions={0}, use_global_device_ids=true | all-gather | bytes 149952 | tf_op jit(solution)/shard_map/all_gather | solution.py:64
  49.0 0.3 reshape.350
  49.4 0.7 gather_fusion.1
  51.3 3.5 fusion.96
  55.1 0.4 fusion.95
  55.5 0.8 concatenate.40
  56.5 0.6 gather_fusion
  58.3 19.3 %all-reduce.3.cloned.1.call-done = f32[16,1548]{1,0:T(8,128)} async-done(((f32[16,1548]{1,0:T(8,128)}), f32[16,1548]{1,0:T(8,128)}) %all-reduce.3.cloned.1.call-update) | async-done | bytes 99088 | tf_op jit(solution)/shard_map/psum | solution.py:73
  77.6 0.8 slice.99
  78.4 0.7 slice.121
  79.4 32.2 %all_gather.17 = bf16[4,2,4544]{0,1,2:T(2,128)(2,1)} all-gather(bf16[4,2,284]{0,1,2:T(2,128)(2,1)S(1)} %copy.92), channel_id=1, replica_groups=mesh['req'=2,'seq'=16] {'seq'}, dimensions={2}, use_global_device_ids=true | all-gather | bytes 77248 | tf_op jit(solution)/shard_map/all_gather | solution.py:80
  111.6 5.2 %copy.73 = bf16[4,2,4544]{2,0,1:T(4,128)(2,1)S(1)} copy(bf16[4,2,4544]{0,1,2:T(2,128)(2,1)} %all_gather.17) | data formatting | bytes 145408 | tf_op jit(solution)/shard_map/all_gather | solution.py:80
  118.8 0.5 select_reduce_fusion
  119.3 41.3 %pmax.7 = f32[4,284]{1,0:T(4,128)S(1)} all-reduce(f32[4,284]{1,0:T(4,128)S(1)} %constant_dynamic-update-slice_fusion), channel_id=1, replica_groups=mesh['req'=2,'seq'=16] {'req','seq'}, use_global_device_ids=true, to_apply=%region_5.6 | all-reduce | flops 1136 | bytes 9088 | tf_op jit(solution)/shard_map/pmax | solution.py:121
  160.6 0.4 fusion
  161.0 0.4 convolution_multiply_fusion.1
  161.7 0.8 copy-done.2
  162.6 0.8 scatter_custom_fusion
  163.4 97.1 %all-gather.3.cloned.1.call-done = f32[32,4,284,65]{2,1,3,0:T(4,128)} async-done(((f32[1,4,284,65]{2,1,3,0:T(4,128)}), f32[32,4,284,65]{2,1,3,0:T(4,128)}) %all-gather.3.cloned.1.call-update) | async-done | bytes 9451536 | tf_op jit(solution)/shard_map/all_gather | solution.py:131
  260.5 6.7 %reduce_sum.39 = f32[4,284,65]{1,0,2:T(4,128)S(1)} reduce(f32[32,4,284,65]{2,1,3,0:T(4,128)} %all-gather.3.cloned.1.call-done, f32[]{:T(128)} %constant.57.clone.1), dimensions={0}, to_apply=%region_7.8 | reduce | flops 2289040 | bytes 9746884 | tf_op jit(solution)/shard_map/reduce_sum | solution.py:131
  267.9 0.4 fusion.55
  268.4 3.4 convolution_add_fusion
  271.9 1.3 dynamic_update_slice.12
  273.3 0.8 copy.86
  274.3 0.8 copy.88
  275.1 125.5 %all-reduce.5.cloned.1.call-done = f32[4,4,4544]{2,0,1:T(4,128)} async-done(((f32[4,4,4544]{2,0,1:T(4,128)}), f32[4,4,4544]{2,0,1:T(4,128)}) %all-reduce.5.cloned.1.call-update) | async-done | bytes 290832 | tf_op jit(solution)/shard_map/psum | solution.py:148
  400.6 1.6 gather_fusion.2
  402.3 0.6 copy.87
  (99 shorter events, 6.5 us)
Async XLA Ops:
  7.2 260.7 %copy-start = (bf16[284,2272]{1,0:T(8,128)(2,1)S(1)}, bf16[284,2272]{1,0:T(8,128)(2,1)}, u32[]{:S(2)}) copy-start(bf16[284,2272]{1,0:T(8,128)(2,1)} %param.19) | copy-start | bytes 3871492
  7.2 70.4 %all-reduce.3.cloned.1.call-start = ((), (), s32[]{:S(2)}) async-start(), calls=%async_computation | async-start | bytes 212992 | tf_op jit(solution)/shard_map/psum | solution.py:73
  51.3 3.5 copy-start.4
  51.3 3.8 copy-start.3
  54.8 1.6 copy-start.8
  54.8 1.7 copy-start.1
  55.1 2.6 copy-start.5
  56.3 204.2 %all-gather.3.cloned.1.call-start = ((), (), s32[]{:S(2)}) async-start(), calls=%async_computation.1 | async-start | bytes 13178880 | tf_op jit(solution)/shard_map/all_gather | solution.py:131
  161.7 0.8 copy-start.2
  162.5 238.1 %all-reduce.5.cloned.1.call-start = ((), (), s32[]{:S(2)}) async-start(), calls=%async_computation.2 | async-start | bytes 589824 | tf_op jit(solution)/shard_map/psum | solution.py:148
  267.5 0.9 copy-start.6
  273.2 129.0 %copy-start.7 = (bf16[4,2,284]{2,1,0:T(2,128)(2,1)S(1)}, bf16[4,2,284]{2,1,0:T(2,128)(2,1)}, u32[]{:S(2)}) copy-start(bf16[4,2,284]{2,1,0:T(2,128)(2,1)} %param.11) | copy-start | bytes 13636
Sparse Core Ops, SparseCore 0:
  56.4 21.1 all-reduce.2
  162.7 97.7 all-gather.2
  274.3 126.2 all-reduce.4
